TPU v7x, 256 devices: a whole 4x4x8 slice. The times are simulated.
256 devices in a mesh: dp: 8 (over y, x_hi), shard: 32 (over x_lo, z, core).
Axes of the slice: x: 4 (x_hi: 2, x_lo: 2; x = x_hi * 2 + x_lo), y: 4, z: 8, core: 2. Of those that a mesh axis runs over, the one named last changes fastest.
Arguments:
- grads: float32 [8, 1, 2, 4096, 4096], P('dp', None, None, None, 'shard'), may hold values from -6 to 6
- params: float32 [1, 2, 4096, 4096], P(None, None, ('dp', 'shard')), may hold values from -0.09375 to 0.09375
- moment_one: float32 [1, 2, 4096, 4096], P(None, None, ('dp', 'shard')), may hold values from -0.75 to 0.75
- moment_two: float32 [1, 2, 4096, 4096], P(None, None, ('dp', 'shard')), may hold values from 1e-05 to 0.01
- relation_ids: int32 [1], replicated, may hold values from 0 to 63
- rates: float32 [64], replicated, may hold values from 0.02 to 0.1
- step_count: int32 [1], replicated, may hold values from 1 to 8
Outputs:
- new_params: float32 [1, 2, 4096, 4096], P(None, None, ('dp', 'shard'))
- new_moment_one: float32 [1, 2, 4096, 4096], P(None, None, ('dp', 'shard'))
- new_moment_two: float32 [1, 2, 4096, 4096], P(None, None, ('dp', 'shard'))
- panels: bfloat16 [1, 2, 4096, 4096], P(None, None, None, 'shard')
Inputs may be any that keep to these rules, and one draw needn't show every extreme that they name: `relation_ids`: relation ids are edge types. `step_count`: the step count is positive.
All inputs are finite; a program needn't handle non-finite values.
Results may differ from a plain program's by a relative error of at most 0.001.
Values may be sent and summed in bfloat16 or wider, within the bound.
No kernel may reach another device: no remote copies, remote signals or barrier semaphores. Data moves between devices by JAX's collectives and lax.ppermute only.
A program may use at most 128 MiB of HBM per device.

v0:
```python
import jax
import jax.numpy as jnp
from jax import lax
from jax.sharding import PartitionSpec as P


def body(grads, params, moment_one, moment_two, relation_ids, rates, step_count):
    groups = lax.axis_size("dp")
    owners = lax.axis_size("shard")
    relations = grads.shape[1]
    panel_cols = grads.shape[-1]
    width = panel_cols * owners
    owned = params.shape[2]
    pieces = grads.reshape(relations, 2, groups, owners, owned, panel_cols)
    moved = lax.all_to_all(pieces, "shard", split_axis=3, concat_axis=5, tiled=True)
    summed = lax.psum_scatter(moved, "dp", scatter_dimension=2, tiled=True)
    gradient = summed.reshape(relations, 2, owned, width) / groups
    onehot = (relation_ids[:, None] == jnp.arange(rates.shape[0], dtype=jnp.int32)[None, :]).astype(
        jnp.float32
    )
    learn = jnp.sum(onehot * rates[None, :], axis=1)[:, None, None, None]
    new_one = 0.9 * moment_one + 0.1 * gradient
    new_two = 0.95 * moment_two + 0.05 * gradient * gradient
    steps = step_count[0].astype(jnp.float32)
    fix_one = 1.0 - jnp.power(jnp.float32(0.9), steps)
    fix_two = 1.0 - jnp.power(jnp.float32(0.95), steps)
    update = new_one / fix_one / (jnp.sqrt(new_two / fix_two) + 1e-08) + 0.1 * params
    new_params = params - learn * update
    fresh = new_params.astype(jnp.bfloat16).reshape(relations, 2, 1, 1, owned, width)
    stacked = lax.all_gather(fresh, "dp", axis=2, tiled=True)
    panel = lax.all_to_all(stacked, "shard", split_axis=5, concat_axis=3, tiled=True)
    panels = panel.reshape(relations, 2, width, panel_cols)
    return (new_params, new_one, new_two, panels)


def solution(mesh):
    in_specs = (
        P("dp", None, None, None, "shard"),
        P(None, None, ("dp", "shard"), None),
        P(None, None, ("dp", "shard"), None),
        P(None, None, ("dp", "shard"), None),
        P(),
        P(),
        P(),
    )
    out_specs = (
        P(None, None, ("dp", "shard"), None),
        P(None, None, ("dp", "shard"), None),
        P(None, None, ("dp", "shard"), None),
        P(None, None, None, "shard"),
    )
    return jax.shard_map(body, mesh=mesh, in_specs=in_specs, out_specs=out_specs, check_vma=False)
```

profile of v0, /device:TPU:32, one launch (start us, length us, event | category | flops | bytes accessed | tf_op | source)
XLA Modules:
  0.0 405.4 jit_solution(11220922597998962744)
XLA Ops:
  7.2 0.0 reduce-scatter.2.cloned.1.call-start
  7.2 2.8 copy.31
  10.1 105.8 %all_to_all.33 = f32[1,2,8,32,16,128]{5,4,1,2,0,3:T(8,128)S(1)} all-to-all(f32[1,2,8,32,16,128]{5,4,1,2,0,3:T(8,128)S(1)} %copy.31), channel_id=1, replica_groups=mesh['dp'=8,'shard'=32] {'shard'}, dimensions={3} | all-to-all | bytes 8388608 | tf_op jit(solution)/shard_map/all_to_all | solution.py:15
  115.9 2.4 copy.32
  118.3 5.7 %copy.33 = f32[1,2,8,1,16,4096]{5,4,3,1,0,2:T(8,128)} copy(f32[1,2,8,1,16,4096]{5,3,4,2,1,0:T(1,128)S(1)} %bitcast.38) | data formatting | bytes 8388608 | tf_op jit(solution)/shard_map/all_to_all | solution.py:15
  124.0 0.0 copy-start.3
  124.0 0.0 copy-start
  124.0 0.0 copy-start.1
  124.0 0.0 copy-start.2
  124.1 0.0 reduce-scatter.2.cloned.1.call-update
  124.1 0.0 all-gather.3.cloned.1.call-start
  125.6 0.0 copy-done.3
  125.6 0.7 fusion.1
  126.3 85.0 %reduce-scatter.2.cloned.1.call-done = f32[1,2,1,1,16,4096]{5,4,3,1,0,2:T(8,128)} async-done(((f32[1,2,8,1,16,4096]{5,4,3,1,0,2:T(8,128)}), f32[1,2,1,1,16,4096]{5,4,3,1,0,2:T(8,128)}) %reduce-scatter.2.cloned.1.call-update) | async-done | bytes 524304 | tf_op jit(solution)/shard_map/reduce_scatter | solution.py:16
  211.3 0.0 copy-done
  211.3 0.0 copy-done.1
  211.3 0.0 copy-done.2
  211.3 3.2 fusion.2
  214.5 0.0 all-gather.3.cloned.1.call-update
  214.6 57.6 %all-gather.3.cloned.1.call-done = bf16[1,2,128,4096]{3,2,1,0:T(8,128)(2,1)} async-done(((bf16[1,2,16,4096]{3,2,1,0:T(8,128)(2,1)}), bf16[1,2,128,4096]{3,2,1,0:T(8,128)(2,1)}) %all-gather.3.cloned.1.call-update) | async-done | bytes 2097168 | tf_op jit(solution)/shard_map/all_gather | solution.py:30
  272.1 15.3 %copy.37 = bf16[1,2,8,1,16,4096]{4,2,1,3,0,5:T(8,128)(2,1)} copy(bf16[1,2,8,1,16,4096]{5,4,2,1,3,0:T(8,128)(2,1)} %bitcast.41) | data formatting | bytes 4194304 | tf_op jit(solution)/shard_map/all_gather | solution.py:30
  287.4 19.7 %reshape.90 = bf16[32,2,16384]{2,1,0:T(2,128)(2,1)S(1)} reshape(bf16[4096,1,1,2,8,16]{5,4,3,2,1,0:T(8,128)(2,1)} %bitcast.36) | data formatting | bytes 4194304
  307.2 59.0 %all_to_all.34 = bf16[32,2,16384]{2,1,0:T(2,128)(2,1)} all-to-all(bf16[32,2,16384]{2,1,0:T(2,128)(2,1)S(1)} %reshape.90), channel_id=1, replica_groups=mesh['dp'=8,'shard'=32] {'shard'}, dimensions={0} | all-to-all | bytes 4194304 | tf_op jit(solution)/shard_map/all_to_all | solution.py:31
  366.2 16.4 %reshape.91 = bf16[4096,1,1,2,8,16]{5,4,3,2,1,0:T(8,128)(2,1)} reshape(bf16[32,2,16384]{2,1,0:T(2,128)(2,1)} %all_to_all.34) | data formatting | bytes 4194304
  382.6 13.7 %copy.40 = bf16[1,2,8,1,16,32,128]{6,5,4,2,1,3,0:T(8,128)(2,1)S(1)} copy(bf16[1,2,8,1,16,32,128]{4,2,1,6,5,3,0:T(8,128)(2,1)} %bitcast.37) | data formatting | bytes 4194304 | tf_op jit(solution)/shard_map/all_to_all | solution.py:31
  396.4 2.2 copy.39
Async XLA Ops:
  7.2 204.2 %reduce-scatter.2.cloned.1.call-start = ((), (), s32[]{:S(2)}) async-start(), calls=%async_computation.3 | async-start | bytes 4718592 | tf_op jit(solution)/shard_map/reduce_scatter | solution.py:16
  124.0 1.6 copy-start.3
  124.0 87.3 %copy-start = (f32[1,2,16,4096]{3,2,1,0:T(8,128)S(1)}, f32[1,2,16,4096]{3,2,1,0:T(8,128)}, u32[]{:S(2)}) copy-start(f32[1,2,16,4096]{3,2,1,0:T(8,128)} %param.8) | copy-start | bytes 1572868
  124.0 87.3 %copy-start.1 = (f32[1,2,16,4096]{3,2,1,0:T(8,128)S(1)}, f32[1,2,16,4096]{3,2,1,0:T(8,128)}, u32[]{:S(2)}) copy-start(f32[1,2,16,4096]{3,2,1,0:T(8,128)} %param.10) | copy-start | bytes 1572868
  124.0 87.3 %copy-start.2 = (f32[1,2,16,4096]{3,2,1,0:T(8,128)S(1)}, f32[1,2,16,4096]{3,2,1,0:T(8,128)}, u32[]{:S(2)}) copy-start(f32[1,2,16,4096]{3,2,1,0:T(8,128)} %param.9) | copy-start | bytes 1572868
  124.1 148.1 %all-gather.3.cloned.1.call-start = ((), (), s32[]{:S(2)}) async-start(), calls=%async_computation.4 | async-start | bytes 2359296 | tf_op jit(solution)/shard_map/all_gather | solution.py:30
Sparse Core Ops, SparseCore 0:
  124.2 87.0 reduce-scatter.1
  214.7 57.4 all-gather.2
where the time goes:
time: 407 us; the launch traced here: 405 us
  blocking collectives  165 us (41%)
  waiting for transfers between devices  143 us (35%)
  local copies, waits for them, and re-layouts  78.4 us (19%)
  between operations  15.6 us (4%)
    all_to_all x1, blocking collectives, body(): lax.all_to_all(pieces, 'shard', split_axis=3, concat_axis=5, tiled=True)  106 us
    reduce_scatter x1, waiting for transfers between devices, body(): summed = lax.psum_scatter(moved, 'dp', scatter_dimension=2, tiled=True)  85 us
    all_to_all x1, blocking collectives, body(): lax.all_to_all(stacked, 'shard', split_axis=5, concat_axis=3, tiled=True)  59 us
    all_gather x1, waiting for transfers between devices, body(): stacked = lax.all_gather(fresh, 'dp', axis=2, tiled=True)  57.6 us
    unnamed x10, local copies, waits for them, and re-layouts  36.2 us
    all_to_all x2, local copies, waits for them, and re-layouts, body(): lax.all_to_all(stacked, 'shard', split_axis=5, concat_axis=3, tiled=True)  15.9 us
    all_gather x1, local copies, waits for them, and re-layouts, body(): stacked = lax.all_gather(fresh, 'dp', axis=2, tiled=True)  15.3 us
    all_to_all x2, local copies, waits for them, and re-layouts, body(): lax.all_to_all(pieces, 'shard', split_axis=3, concat_axis=5, tiled=True)  8.15 us
  transfers between devices with their start and end apart: 2, of which 2 were waited for; matrix products, arithmetic and copies ran while one was open for 0% of the time, Pallas kernels for 0%

commit v1 on v0

--- a/solution.py
+++ b/solution.py
@@ -27,7 +27,9 @@
     update = new_one / fix_one / (jnp.sqrt(new_two / fix_two) + 1e-08) + 0.1 * params
     new_params = params - learn * update
     fresh = new_params.astype(jnp.bfloat16).reshape(relations, 2, 1, 1, owned, width)
-    stacked = lax.all_gather(fresh, "dp", axis=2, tiled=True)
+    stacked = jnp.concatenate(
+        lax.all_to_all(jnp.stack([fresh] * lax.axis_size("dp")), "dp", 0, 0), axis=2
+    )
     panel = lax.all_to_all(stacked, "shard", split_axis=5, concat_axis=3, tiled=True)
     panels = panel.reshape(relations, 2, width, panel_cols)
     return (new_params, new_one, new_two, panels)

time: 407 us -> 379 us (0.931)
  waiting for transfers between devices: 143 us -> 85.1 us
  blocking collectives: 165 us -> 196 us
    all_gather x1 -> x0, waiting for transfers between devices: 57.6 us -> none  [body(): stacked = lax.all_gather(fresh, 'dp', axis=2, tiled=True)]
    all_to_all x0 -> x1, blocking collectives: none -> 30.3 us  [body(): lax.all_to_all(jnp.stack([fresh] * lax.axis_size('dp')), 'dp', 0, 0)]
    all_gather x1 -> x0, local copies, waits for them, and re-layouts: 15.3 us -> none  [body(): stacked = lax.all_gather(fresh, 'dp', axis=2, tiled=True)]
    reshape x0 -> x1, local copies, waits for them, and re-layouts: none -> 14 us  [body(): jnp.concatenate(lax.all_to_all(jnp.stack([fresh] * lax.axis_size('dp')),...]
  transfers between devices with their start and end apart: 2 -> 1, of which waited for: 2 -> 1; matrix products, arithmetic and copies ran while one was open for 0% -> 0% of each run, Pallas kernels for 0% -> 0%
where the time goes in v1:
time: 379 us; the launch traced here: 378 us
  blocking collectives  196 us (52%)
  waiting for transfers between devices  85.1 us (22%)
  local copies, waits for them, and re-layouts  77.4 us (20%)
  between operations  15.6 us (4%)
    all_to_all x1, blocking collectives, body(): lax.all_to_all(pieces, 'shard', split_axis=3, concat_axis=5, tiled=True)  106 us
    reduce_scatter x1, waiting for transfers between devices, body(): summed = lax.psum_scatter(moved, 'dp', scatter_dimension=2, tiled=True)  85.1 us
    all_to_all x1, blocking collectives, body(): lax.all_to_all(stacked, 'shard', split_axis=5, concat_axis=3, tiled=True)  59.8 us
    unnamed x10, local copies, waits for them, and re-layouts  36.2 us
    all_to_all x1, blocking collectives, body(): lax.all_to_all(jnp.stack([fresh] * lax.axis_size('dp')), 'dp', 0, 0)  30.3 us
    all_to_all x2, local copies, waits for them, and re-layouts, body(): lax.all_to_all(stacked, 'shard', split_axis=5, concat_axis=3, tiled=True)  15.9 us
    reshape x1, local copies, waits for them, and re-layouts, body(): jnp.concatenate(lax.all_to_all(jnp.stack([fresh] * lax.axis_size('dp')),...  14 us
    all_to_all x2, local copies, waits for them, and re-layouts, body(): lax.all_to_all(pieces, 'shard', split_axis=3, concat_axis=5, tiled=True)  8.16 us
  transfers between devices with their start and end apart: 1, of which 1 were waited for; matrix products, arithmetic and copies ran while one was open for 0% of the time, Pallas kernels for 0%

profile of v1, /device:TPU:32, one launch (start us, length us, event | category | flops | bytes accessed | tf_op | source)
XLA Modules:
  0.0 377.7 jit_solution(16755498019997602773)
XLA Ops:
  7.2 0.0 reduce-scatter.2.cloned.1.call-start
  7.2 2.8 copy.31
  10.1 105.8 %all_to_all.38 = f32[1,2,8,32,16,128]{5,4,1,2,0,3:T(8,128)S(1)} all-to-all(f32[1,2,8,32,16,128]{5,4,1,2,0,3:T(8,128)S(1)} %copy.31), channel_id=1, replica_groups=mesh['dp'=8,'shard'=32] {'shard'}, dimensions={3} | all-to-all | bytes 8388608 | tf_op jit(solution)/shard_map/all_to_all | solution.py:15
  115.9 2.4 copy.32
  118.3 5.7 %copy.33 = f32[1,2,8,1,16,4096]{5,4,3,1,0,2:T(8,128)} copy(f32[1,2,8,1,16,4096]{5,3,4,2,1,0:T(1,128)S(1)} %bitcast.33) | data formatting | bytes 8388608 | tf_op jit(solution)/shard_map/all_to_all | solution.py:15
  124.0 0.0 copy-start.3
  124.0 0.0 copy-start
  124.0 0.0 copy-start.1
  124.0 0.0 copy-start.2
  124.1 0.0 reduce-scatter.2.cloned.1.call-update
  125.6 0.0 copy-done.3
  125.6 0.7 fusion
  126.2 85.1 %reduce-scatter.2.cloned.1.call-done = f32[1,2,1,1,16,4096]{5,4,3,1,0,2:T(8,128)} async-done(((f32[1,2,8,1,16,4096]{5,4,3,1,0,2:T(8,128)}), f32[1,2,1,1,16,4096]{5,4,3,1,0,2:T(8,128)}) %reduce-scatter.2.cloned.1.call-update) | async-done | bytes 524304 | tf_op jit(solution)/shard_map/reduce_scatter | solution.py:16
  211.3 0.0 copy-done
  211.3 0.0 copy-done.1
  211.3 0.0 copy-done.2
  211.3 3.1 convert_bitcast_fusion
  214.4 0.2 stack.3
  214.6 30.3 %all_to_all.39 = bf16[8,1,2,1,1,16,4096]{6,5,2,4,3,1,0:T(8,128)(2,1)S(1)} all-to-all(bf16[8,1,2,1,1,16,4096]{6,5,2,4,3,1,0:T(8,128)(2,1)S(1)} %stack.3), channel_id=1, replica_groups=mesh['dp'=8,'shard'=32] {'dp'}, dimensions={0} | all-to-all | bytes 4194304 | tf_op jit(solution)/shard_map/all_to_all | solution.py:31
  244.9 14.0 %copy.35 = bf16[1,2,8,1,16,4096]{4,2,1,3,0,5:T(8,128)(2,1)} copy(bf16[1,2,8,1,16,4096]{5,4,1,2,3,0:T(8,128)(2,1)S(1)} %bitcast.34) | data formatting | bytes 4194304 | tf_op jit(solution)/shard_map/reshape | solution.py:30
  258.9 19.7 %reshape.96 = bf16[32,2,16384]{2,1,0:T(2,128)(2,1)S(1)} reshape(bf16[4096,1,1,2,8,16]{5,4,3,2,1,0:T(8,128)(2,1)} %bitcast.31) | data formatting | bytes 4194304
  278.6 59.8 %all_to_all.40 = bf16[32,2,16384]{2,1,0:T(2,128)(2,1)} all-to-all(bf16[32,2,16384]{2,1,0:T(2,128)(2,1)S(1)} %reshape.96), channel_id=1, replica_groups=mesh['dp'=8,'shard'=32] {'shard'}, dimensions={0} | all-to-all | bytes 4194304 | tf_op jit(solution)/shard_map/all_to_all | solution.py:33
  338.5 16.5 %reshape.97 = bf16[4096,1,1,2,8,16]{5,4,3,2,1,0:T(8,128)(2,1)} reshape(bf16[32,2,16384]{2,1,0:T(2,128)(2,1)} %all_to_all.40) | data formatting | bytes 4194304
  355.0 13.7 %copy.38 = bf16[1,2,8,1,16,32,128]{6,5,4,2,1,3,0:T(8,128)(2,1)S(1)} copy(bf16[1,2,8,1,16,32,128]{4,2,1,6,5,3,0:T(8,128)(2,1)} %bitcast.32) | data formatting | bytes 4194304 | tf_op jit(solution)/shard_map/all_to_all | solution.py:33
  368.7 2.2 copy.37
Async XLA Ops:
  7.2 204.2 %reduce-scatter.2.cloned.1.call-start = ((), (), s32[]{:S(2)}) async-start(), calls=%async_computation.4 | async-start | bytes 4718592 | tf_op jit(solution)/shard_map/reduce_scatter | solution.py:16
  124.0 1.5 copy-start.3
  124.0 87.3 %copy-start = (f32[1,2,16,4096]{3,2,1,0:T(8,128)S(1)}, f32[1,2,16,4096]{3,2,1,0:T(8,128)}, u32[]{:S(2)}) copy-start(f32[1,2,16,4096]{3,2,1,0:T(8,128)} %param.8) | copy-start | bytes 1572868
  124.0 87.3 %copy-start.1 = (f32[1,2,16,4096]{3,2,1,0:T(8,128)S(1)}, f32[1,2,16,4096]{3,2,1,0:T(8,128)}, u32[]{:S(2)}) copy-start(f32[1,2,16,4096]{3,2,1,0:T(8,128)} %param.10) | copy-start | bytes 1572868
  124.0 87.3 %copy-start.2 = (f32[1,2,16,4096]{3,2,1,0:T(8,128)S(1)}, f32[1,2,16,4096]{3,2,1,0:T(8,128)}, u32[]{:S(2)}) copy-start(f32[1,2,16,4096]{3,2,1,0:T(8,128)} %param.9) | copy-start | bytes 1572868
Sparse Core Ops, SparseCore 0:
  124.2 87.0 reduce-scatter.1

commit v2 on v0

--- a/solution.py
+++ b/solution.py
@@ -28,7 +28,12 @@
     new_params = params - learn * update
     fresh = new_params.astype(jnp.bfloat16).reshape(relations, 2, 1, 1, owned, width)
     stacked = lax.all_gather(fresh, "dp", axis=2, tiled=True)
-    panel = lax.all_to_all(stacked, "shard", split_axis=5, concat_axis=3, tiled=True)
+    panel = jnp.concatenate(
+        lax.all_to_all(
+            jnp.stack(jnp.split(stacked, lax.axis_size("shard"), axis=5)), "shard", 0, 0
+        ),
+        axis=3,
+    )
     panels = panel.reshape(relations, 2, width, panel_cols)
     return (new_params, new_one, new_two, panels)
 

time: 407 us -> 355 us (0.87)
  local copies, waits for them, and re-layouts: 78.4 us -> 27.1 us
    unnamed x10 -> x41, local copies, waits for them, and re-layouts: 36.2 us -> 14.2 us
    all_gather x1 -> x0, local copies, waits for them, and re-layouts: 15.3 us -> none  [body(): stacked = lax.all_gather(fresh, 'dp', axis=2, tiled=True)]
    all_to_all x2 -> x1, local copies, waits for them, and re-layouts: 15.9 us -> 1.86 us  [body(): lax.all_to_all(jnp.stack(jnp.split(stacked, lax.axis_size('shard'), axis=...]
where the time goes in v2:
time: 355 us; the launch traced here: 354 us
  blocking collectives  165 us (46%)
  waiting for transfers between devices  143 us (40%)
  local copies, waits for them, and re-layouts  27.1 us (8%)
  between operations  15.6 us (4%)
  other arithmetic  3.88 us (1%)
    all_to_all x1, blocking collectives, body(): lax.all_to_all(pieces, 'shard', split_axis=3, concat_axis=5, tiled=True)  106 us
    reduce_scatter x1, waiting for transfers between devices, body(): summed = lax.psum_scatter(moved, 'dp', scatter_dimension=2, tiled=True)  85 us
    all_to_all x1, blocking collectives, body(): lax.all_to_all(jnp.stack(jnp.split(stacked, lax.axis_size('shard'), axis=...  58.9 us
    all_gather x1, waiting for transfers between devices, body(): stacked = lax.all_gather(fresh, 'dp', axis=2, tiled=True)  57.6 us
    unnamed x41, local copies, waits for them, and re-layouts  14.2 us
    all_to_all x2, local copies, waits for them, and re-layouts, body(): lax.all_to_all(pieces, 'shard', split_axis=3, concat_axis=5, tiled=True)  8.17 us
  transfers between devices with their start and end apart: 2, of which 2 were waited for; matrix products, arithmetic and copies ran while one was open for 0% of the time, Pallas kernels for 0%

profile of v2, /device:TPU:32, one launch (start us, length us, event | category | flops | bytes accessed | tf_op | source)
XLA Modules:
  0.0 354.1 jit_solution(9489471789073494876)
XLA Ops:
  7.2 0.0 reduce-scatter.2.cloned.1.call-start
  7.2 2.8 copy.54
  10.1 105.8 %all_to_all.23 = f32[1,2,8,32,16,128]{5,4,1,2,0,3:T(8,128)S(1)} all-to-all(f32[1,2,8,32,16,128]{5,4,1,2,0,3:T(8,128)S(1)} %copy.54), channel_id=1, replica_groups=mesh['dp'=8,'shard'=32] {'shard'}, dimensions={3} | all-to-all | bytes 8388608 | tf_op jit(solution)/shard_map/all_to_all | solution.py:15
  115.9 2.4 copy.55
  118.3 5.7 %copy.56 = f32[1,2,8,1,16,4096]{5,4,3,1,0,2:T(8,128)} copy(f32[1,2,8,1,16,4096]{5,3,4,2,1,0:T(1,128)S(1)} %bitcast.153) | data formatting | bytes 8388608 | tf_op jit(solution)/shard_map/all_to_all | solution.py:15
  124.1 0.0 reduce-scatter.2.cloned.1.call-update
  124.1 0.0 all-gather.3.cloned.1.call-start
  125.6 0.0 copy-done.4
  125.6 0.7 fusion
  126.3 85.0 %reduce-scatter.2.cloned.1.call-done = f32[1,2,1,1,16,4096]{5,4,3,1,0,2:T(8,128)} async-done(((f32[1,2,8,1,16,4096]{5,4,3,1,0,2:T(8,128)}), f32[1,2,1,1,16,4096]{5,4,3,1,0,2:T(8,128)}) %reduce-scatter.2.cloned.1.call-update) | async-done | bytes 524304 | tf_op jit(solution)/shard_map/reduce_scatter | solution.py:16
  211.3 0.0 copy-done.2
  211.4 3.2 fusion.1
  214.6 0.0 all-gather.3.cloned.1.call-update
  214.6 57.6 %all-gather.3.cloned.1.call-done = bf16[1,2,128,4096]{3,2,1,0:T(8,128)(2,1)} async-done(((bf16[1,2,16,4096]{3,2,1,0:T(8,128)(2,1)}), bf16[1,2,128,4096]{3,2,1,0:T(8,128)(2,1)}) %all-gather.3.cloned.1.call-update) | async-done | bytes 2097168 | tf_op jit(solution)/shard_map/all_gather | solution.py:30
  272.2 1.0 constant_dynamic-update-slice_fusion.31
  273.1 0.9 constant_dynamic-update-slice_fusion.30
  274.0 0.9 constant_dynamic-update-slice_fusion.29
  274.9 0.9 constant_dynamic-update-slice_fusion.28
  275.7 0.9 constant_dynamic-update-slice_fusion.27
  276.6 0.9 constant_dynamic-update-slice_fusion.26
  277.4 0.9 constant_dynamic-update-slice_fusion.25
  278.3 0.9 constant_dynamic-update-slice_fusion.24
  279.1 0.9 constant_dynamic-update-slice_fusion.23
  280.0 0.9 constant_dynamic-update-slice_fusion.22
  280.8 0.9 constant_dynamic-update-slice_fusion.21
  281.7 0.9 constant_dynamic-update-slice_fusion.20
  282.5 0.9 constant_dynamic-update-slice_fusion.19
  283.4 0.9 constant_dynamic-update-slice_fusion.18
  284.3 0.9 constant_dynamic-update-slice_fusion.17
  285.1 0.9 constant_dynamic-update-slice_fusion.16
  286.5 58.9 %all_to_all.24 = bf16[32,1,2,8,1,16,128]{6,5,3,2,4,1,0:T(8,128)(2,1)S(1)} all-to-all(bf16[32,1,2,8,1,16,128]{6,5,3,2,4,1,0:T(8,128)(2,1)S(1)} %constant_dynamic-update-slice_fusion), channel_id=1, replica_groups=mesh['dp'=8,'shard'=32] {'shard'}, dimensions={0} | all-to-all | bytes 4194304 | tf_op jit(solution)/shard_map/all_to_all | solution.py:32
  345.4 1.9 copy.58
  (24 shorter events, 0.5 us)
Async XLA Ops:
  7.2 204.2 %reduce-scatter.2.cloned.1.call-start = ((), (), s32[]{:S(2)}) async-start(), calls=%async_computation.3 | async-start | bytes 4718592 | tf_op jit(solution)/shard_map/reduce_scatter | solution.py:16
  124.1 1.6 copy-start.4
  124.1 87.3 %copy-start.1 = (f32[1,2,16,4096]{3,2,1,0:T(8,128)S(1)}, f32[1,2,16,4096]{3,2,1,0:T(8,128)}, u32[]{:S(2)}) copy-start(f32[1,2,16,4096]{3,2,1,0:T(8,128)} %param.8) | copy-start | bytes 1572868
  124.1 87.3 %copy-start.2 = (f32[1,2,16,4096]{3,2,1,0:T(8,128)S(1)}, f32[1,2,16,4096]{3,2,1,0:T(8,128)}, u32[]{:S(2)}) copy-start(f32[1,2,16,4096]{3,2,1,0:T(8,128)} %param.10) | copy-start | bytes 1572868
  124.1 87.3 %copy-start.3 = (f32[1,2,16,4096]{3,2,1,0:T(8,128)S(1)}, f32[1,2,16,4096]{3,2,1,0:T(8,128)}, u32[]{:S(2)}) copy-start(f32[1,2,16,4096]{3,2,1,0:T(8,128)} %param.9) | copy-start | bytes 1572868
  124.1 148.1 %all-gather.3.cloned.1.call-start = ((), (), s32[]{:S(2)}) async-start(), calls=%async_computation.4 | async-start | bytes 2359296 | tf_op jit(solution)/shard_map/all_gather | solution.py:30
  272.2 13.8 %copy-start = (bf16[1,2,128,4096]{3,2,1,0:T(8,128)(2,1)S(1)}, bf16[1,2,128,4096]{3,2,1,0:T(8,128)(2,1)}, u32[]{:S(2)}) copy-start(bf16[1,2,128,4096]{3,2,1,0:T(8,128)(2,1)} %all-gather.3.cloned.1.call-done) | copy-start | bytes 6291460
Sparse Core Ops, SparseCore 0:
  124.2 87.0 reduce-scatter.1
  214.7 57.4 all-gather.2
